TPU v7x, 256 devices: a whole 4x4x8 slice. The times are simulated.
256 devices in a mesh: seq: 64 (over y, z, core), txt: 4 (over x).
Axes of the slice: x: 4, y: 4, z: 8, core: 2. Of those that a mesh axis runs over, the one named last changes fastest.
Arguments:
- self_q: bfloat16 [24576, 1024], P('seq', 'txt'), may hold values from -8 to 8
- self_k: bfloat16 [24576, 1024], P('seq', 'txt'), may hold values from -8 to 8
- self_v: bfloat16 [24576, 1024], P('seq', 'txt'), may hold values from -6 to 6
- cross_q: bfloat16 [24576, 1024], P('seq', 'txt'), may hold values from -8 to 8
- text_k: bfloat16 [4096, 1024], P('txt'), may hold values from -8 to 8
- text_v: bfloat16 [4096, 1024], P('txt'), may hold values from -6 to 6
- lags: int32 [192], P('seq'), may hold values from 1 to 32, as said below
Outputs:
- self_out: bfloat16 [24576, 1024], P('seq', 'txt')
- cross_out: bfloat16 [24576, 1024], P('seq', 'txt')
Inputs may be any that keep to these rules, and one draw needn't show every extreme that they name: lags never fall from one span to the next; the last span sees all 32 blocks.
All inputs are finite; a program needn't handle non-finite values.
Results may differ from a plain program's by a relative error of at most 0.014.
Values may be sent and summed in bfloat16 or wider, within the bound.
No kernel may reach another device: no remote copies, remote signals or barrier semaphores. Data moves between devices by JAX's collectives and lax.ppermute only.
A program may use at most 128 MiB of HBM per device.

v0:
```python
import math
import jax
import jax.numpy as jnp
from jax import lax
from jax.sharding import PartitionSpec as P

HSIZE = 128
SPAN = 128
TBLK = 128
NEG_FILL = -1e30


def scale_columns(weighted, scale):
    rows = weighted.shape[0]
    heads = scale.shape[0]
    shaped = weighted.reshape(rows, heads, weighted.shape[1] // heads)
    return (shaped * jnp.transpose(scale)[:, :, None]).reshape(rows, weighted.shape[1])


def softmax_update(state, query, keys, values, visible, factor):
    running, totals, weighted = state
    heads = running.shape[0]
    peaks = []
    sums = []
    columns = []
    for head in range(heads):
        low = head * HSIZE
        high = low + HSIZE
        scores = (
            lax.dot_general(
                query[:, low:high],
                keys[:, low:high],
                (((1,), (1,)), ((), ())),
                preferred_element_type=jnp.float32,
            )
            * factor
        )
        scores = jnp.where(visible, scores, NEG_FILL)
        peak = jnp.maximum(running[head], jnp.max(scores, axis=1))
        probs = jnp.where(visible, jnp.exp(scores - peak[:, None]), 0.0)
        shrink = jnp.exp(running[head] - peak)
        sums.append(totals[head] * shrink + jnp.sum(probs, axis=1))
        mixed = jnp.dot(
            probs.astype(jnp.bfloat16), values[:, low:high], preferred_element_type=jnp.float32
        )
        columns.append(weighted[:, low:high] * shrink[:, None] + mixed)
        peaks.append(peak)
    return (jnp.stack(peaks), jnp.stack(sums), jnp.concatenate(columns, axis=1))


def empty_state(heads, rows, width):
    return (
        jnp.full((heads, rows), NEG_FILL, jnp.float32),
        jnp.zeros((heads, rows), jnp.float32),
        jnp.zeros((rows, heads * width), jnp.float32),
    )


def finish(state):
    return scale_columns(state[2], 1.0 / state[1]).astype(jnp.bfloat16)


def per_device(self_q, self_k, self_v, cross_q, text_k, text_v, lags):
    rows = self_q.shape[0]
    half = rows // 2
    local_heads = self_q.shape[1] // HSIZE
    factor = 1.0 / math.sqrt(HSIZE)
    place = lax.axis_index("seq")
    offsets = jnp.arange(half, dtype=jnp.int32)
    lower = self_q[:half]
    upper = self_q[half:]
    upper_pos = place * rows + half + offsets
    positions = [place * rows + offsets, upper_pos]
    groups = [lower, upper]

    def visit(states, key_block, value_block, first, length):
        key_pos = first + jnp.arange(length, dtype=jnp.int32)
        updated = []
        for group in range(2):
            visible = key_pos[None, :] <= positions[group][:, None]
            query = groups[group]
            updated.append(
                lax.cond(
                    first <= positions[group][half - 1],
                    lambda state: softmax_update(
                        state, query, key_block, value_block, visible, factor
                    ),
                    lambda state: state,
                    states[group],
                )
            )
        return tuple(updated)

    initial = (empty_state(local_heads, half, HSIZE), empty_state(local_heads, half, HSIZE))
    carry = initial
    keys = lax.all_gather(self_k, "seq", axis=0, tiled=True)
    values = lax.all_gather(self_v, "seq", axis=0, tiled=True)
    length = keys.shape[0]
    block = 512
    width = keys.shape[1]
    key_blocks = keys.reshape(length // block, block, width)
    value_blocks = values.reshape(length // block, block, width)

    def one_block(states, inputs):
        key_block, value_block, number = inputs
        return (visit(states, key_block, value_block, number * block, block), None)

    carry, _ = lax.scan(
        one_block, carry, (key_blocks, value_blocks, jnp.arange(length // block, dtype=jnp.int32))
    )
    states = carry
    lower_out = finish(states[0])
    upper_out = finish(states[1])
    self_out = jnp.concatenate([lower_out, upper_out], axis=0)
    limits = jnp.repeat(lags * TBLK, SPAN)
    whole_keys, whole_values = (
        lax.all_to_all(text_k, "txt", split_axis=1, concat_axis=0, tiled=True),
        lax.all_to_all(text_v, "txt", split_axis=1, concat_axis=0, tiled=True),
    )
    text_rows = whole_keys.shape[0]
    visible = jnp.arange(text_rows, dtype=jnp.int32)[None, :] < limits[:, None]
    cross_state = softmax_update(
        empty_state(local_heads, rows, HSIZE), cross_q, whole_keys, whole_values, visible, factor
    )
    cross_out = finish(cross_state)
    return (self_out, cross_out)


def solution(mesh):
    return jax.shard_map(
        per_device,
        mesh=mesh,
        in_specs=(
            P("seq", "txt"),
            P("seq", "txt"),
            P("seq", "txt"),
            P("seq", "txt"),
            P("txt", None),
            P("txt", None),
            P("seq"),
        ),
        out_specs=(P("seq", "txt"), P("seq", "txt")),
        check_vma=False,
    )
```

profile of v0, /device:TPU:249, one launch (start us, length us, event | category | flops | bytes accessed | tf_op | source)
XLA Modules:
  0.0 571.9 jit_solution(3053998208419744763)
XLA Ops:
  8.6 3.9 copy.17
  12.6 4.1 all-to-all-start
  16.7 3.9 copy.19
  20.7 21.6 %all-to-all-done = bf16[1024,4,256]{0,2,1:T(8,128)(2,1)S(1)} async-done(((bf16[1024,4,256]{0,2,1:T(8,128)(2,1)}), bf16[1024,4,256]{0,2,1:T(8,128)(2,1)S(1)}, u32[]{:S(2)}, u32[]{:S(2)}) %all-to-all-start) | async-done | bytes 2097184 | tf_op jit(solution)/shard_map/all_to_all | solution.py:117
  42.2 4.6 all-to-all-start.1
  46.9 2.6 copy.18
  49.5 21.9 %all-to-all-done.1 = bf16[1024,4,256]{0,2,1:T(8,128)(2,1)} async-done(((bf16[1024,4,256]{0,2,1:T(8,128)(2,1)}), bf16[1024,4,256]{0,2,1:T(8,128)(2,1)}, u32[]{:S(2)}, u32[]{:S(2)}) %all-to-all-start.1) | async-done | bytes 2097184 | tf_op jit(solution)/shard_map/all_to_all | solution.py:118
  71.5 2.9 copy.20
  74.4 2.8 fusion.83
  78.6 3.3 fusion.48
  81.9 1.6 fusion.59
  83.6 1.6 fusion.56
  86.1 11.4 %all-gather.3.cloned.1.call-done = bf16[24576,256]{1,0:T(8,128)(2,1)} async-done(((bf16[384,256]{1,0:T(8,128)(2,1)}), bf16[24576,256]{1,0:T(8,128)(2,1)}) %all-gather.3.cloned.1.call-update) | async-done | bytes 12582928 | tf_op jit(solution)/shard_map/all_gather | solution.py:96
  97.5 89.2 %all-gather.5.cloned.1.call-done = bf16[24576,256]{1,0:T(8,128)(2,1)} async-done(((bf16[384,256]{1,0:T(8,128)(2,1)}), bf16[24576,256]{1,0:T(8,128)(2,1)}) %all-gather.5.cloned.1.call-update) | async-done | bytes 12582928 | tf_op jit(solution)/shard_map/all_gather | solution.py:97
  186.7 376.7 %while.20 = (s32[]{:T(128)}, f32[2,192]{1,0:T(2,128)S(1)}, f32[2,192]{1,0:T(2,128)S(1)}, f32[192,256]{1,0:T(8,128)S(1)}, f32[2,192]{1,0:T(2,128)S(1)}, /*index=5...) while((s32[]{:T(128)}, f32[2,192]{1,0:T(2,128)S(1)}, ...), condition=%wide.region_13.14_spmd, body=%wide.region_0.13_spmd.sunk | while | flops 206148608 | bytes 8684505 | solution.py:108
  190.2 1.6 conditional.4
  198.0 1.6 conditional.4
  205.9 1.6 conditional.4
  208.6 1.6 conditional.5
  213.7 1.6 conditional.4
  221.6 1.6 conditional.4
  229.4 1.6 conditional.4
  237.3 1.6 conditional.4
  245.1 1.6 conditional.4
  253.0 1.6 conditional.4
  260.8 1.6 conditional.4
  268.7 1.6 conditional.4
  276.5 1.6 conditional.4
  284.4 1.6 conditional.4
  292.2 1.6 conditional.4
  300.1 1.6 conditional.4
  307.9 1.6 conditional.4
  315.8 1.6 conditional.4
  323.6 1.6 conditional.4
  331.5 1.6 conditional.4
  339.3 1.6 conditional.4
  347.2 1.6 conditional.4
  355.0 1.6 conditional.4
  362.9 1.6 conditional.4
  370.7 1.6 conditional.4
  378.6 1.6 conditional.4
  386.4 1.6 conditional.4
  394.3 1.6 conditional.4
  402.1 1.6 conditional.4
  410.0 1.6 conditional.4
  417.8 1.6 conditional.4
  425.7 1.6 conditional.4
  433.5 1.6 conditional.4
  441.3 1.6 conditional.4
  449.2 1.6 conditional.4
  457.0 1.6 conditional.4
  464.9 1.6 conditional.4
  472.7 1.6 conditional.4
  480.6 1.6 conditional.4
  488.4 1.6 conditional.4
  496.3 1.6 conditional.4
  504.1 1.6 conditional.4
  512.0 1.6 conditional.4
  519.8 1.6 conditional.4
  527.7 1.6 conditional.4
  535.5 1.6 conditional.4
  543.4 1.6 conditional.4
  551.2 1.6 conditional.4
  559.1 1.6 conditional.4
  (1384 shorter events, 365.3 us)
Async XLA Ops:
  7.2 90.3 %all-gather.3.cloned.1.call-start = ((), (), s32[]{:S(2)}) async-start(), calls=%async_computation.2 | async-start | bytes 12779520 | tf_op jit(solution)/shard_map/all_gather | solution.py:96
  7.9 178.8 %all-gather.5.cloned.1.call-start = ((), (), s32[]{:S(2)}) async-start(), calls=%async_computation.3 | async-start | bytes 12779520 | tf_op jit(solution)/shard_map/all_gather | solution.py:97
  12.6 34.2 %copy-start.3 = (s32[3]{0:T(128)S(1)}, s32[3]{0:T(128)}, u32[]{:S(2)}) copy-start(s32[3]{0:T(128)} %param.19) | copy-start | bytes 40
  12.6 34.3 %copy-start.1 = (bf16[384,256]{1,0:T(8,128)(2,1)S(1)}, bf16[384,256]{1,0:T(8,128)(2,1)}, u32[]{:S(2)}) copy-start(bf16[384,256]{1,0:T(8,128)(2,1)} %param.13) | copy-start | bytes 589828
  12.6 29.6 %all-to-all-start = ((bf16[1024,4,256]{0,2,1:T(8,128)(2,1)}), bf16[1024,4,256]{0,2,1:T(8,128)(2,1)S(1)}, u32[]{:S(2)}, u32[]{:S(2)}) async-start(bf16[1024,4,256]{0,2,1:T(8,128)(2,1)} %bitcast.57), calls=%async_computation | async-start | bytes 4194304 | tf_op jit(solution)/shard_map/all_to_all | solution.py:117
  42.2 32.2 %copy-start.2 = (bf16[384,256]{1,0:T(8,128)(2,1)S(1)}, bf16[384,256]{1,0:T(8,128)(2,1)}, u32[]{:S(2)}) copy-start(bf16[384,256]{1,0:T(8,128)(2,1)} %param.16) | copy-start | bytes 589828
  42.2 29.3 %all-to-all-start.1 = ((bf16[1024,4,256]{0,2,1:T(8,128)(2,1)}), bf16[1024,4,256]{0,2,1:T(8,128)(2,1)}, u32[]{:S(2)}, u32[]{:S(2)}) async-start(bf16[1024,4,256]{0,2,1:T(8,128)(2,1)} %bitcast.56), calls=%async_computation.1 | async-start | bytes 4194304 | tf_op jit(solution)/shard_map/all_to_all | solution.py:118
  74.4 2.8 copy-start
Sparse Core Ops, SparseCore 0:
  10.7 86.6 all-gather.2
  100.2 86.4 all-gather.4
where the time goes:
time: 574 us; the launch traced here: 572 us
  local copies, waits for them, and re-layouts  149 us (26%)
  waiting for transfers between devices  145 us (25%)
  matrix products  118 us (21%)
  loops' own time  93.5 us (16%)
  other arithmetic  42.7 us (7%)
  between operations  14.3 us (2%)
  starting transfers between devices  8.81 us (2%)
    all_gather x1, waiting for transfers between devices, per_device(): values = lax.all_gather(self_v, 'seq', axis=0, tiled=True)  89.2 us
    another operation x1, loops' own time, per_device(): lax.scan(one_block, carry, (key_blocks, value_blocks, jnp.arange(length /...  86.1 us
    dot_general x194, matrix products, softmax_update(): lax.dot_general(query[:, low:high], keys[:, low:high], (((1,), (1,)), (()...  63.3 us
    dot_general x194, matrix products, softmax_update(): jnp.dot(probs.astype(jnp.bfloat16), values[:, low:high], preferred_elemen...  54.7 us
    slice x96, local copies, waits for them, and re-layouts, visit(): positions[group][half - 1]  53 us
    squeeze x48, local copies, waits for them, and re-layouts, per_device(): lax.scan(one_block, carry, (key_blocks, value_blocks, jnp.arange(length /...  51.4 us
    reduce_sum x97, other arithmetic, softmax_update(): sums.append(totals[head] * shrink + jnp.sum(probs, axis=1))  36 us
    dynamic_slice x48, local copies, waits for them, and re-layouts, per_device(): lax.scan(one_block, carry, (key_blocks, value_blocks, jnp.arange(length /...  29.3 us
  transfers between devices with their start and end apart: 4, of which 4 were waited for; matrix products, arithmetic and copies ran while one was open for 4% of the time, Pallas kernels for 0%

commit v1 on v0

--- a/solution.py
+++ b/solution.py
@@ -3,6 +3,7 @@
 import jax.numpy as jnp
 from jax import lax
 from jax.sharding import PartitionSpec as P
+from jax.lax import all_to_all, axis_size
 
 HSIZE = 128
 SPAN = 128
@@ -94,7 +95,10 @@
     initial = (empty_state(local_heads, half, HSIZE), empty_state(local_heads, half, HSIZE))
     carry = initial
     keys = lax.all_gather(self_k, "seq", axis=0, tiled=True)
-    values = lax.all_gather(self_v, "seq", axis=0, tiled=True)
+    mat_out = axis_size("seq")
+    arr_next = jnp.stack([self_v] * mat_out, axis=0)
+    carry_out = all_to_all(arr_next, concat_axis=0, split_axis=0, axis_name="seq")
+    values = jnp.concatenate(carry_out, axis=0)
     length = keys.shape[0]
     block = 512
     width = keys.shape[1]

time: 574 us -> 799 us (1.39)
  waiting for transfers between devices: 145 us -> 303 us
  blocking collectives: 0 us -> 28.2 us
  local copies, waits for them, and re-layouts: 149 us -> 167 us
    all_to_all x1, waiting for transfers between devices: 21.9 us -> 281 us  [per_device(): all_to_all(arr_next, concat_axis=0, split_axis=0, axis_name='seq')]
    all_gather x1 -> x0, waiting for transfers between devices: 89.2 us -> none  [per_device(): values = lax.all_gather(self_v, 'seq', axis=0, tiled=True)]
    all_to_all x0 -> x1, blocking collectives: none -> 28.2 us  [per_device(): lax.all_to_all(text_v, 'txt', split_axis=1, concat_axis=0, tiled=True)]
    all_gather x1, waiting for transfers between devices: 11.4 us -> 0.01 us  [per_device(): keys = lax.all_gather(self_k, 'seq', axis=0, tiled=True)]
    slice x96, local copies, waits for them, and re-layouts: 53 us -> 61.1 us  [visit(): positions[group][half - 1]]
  transfers between devices with their start and end apart: 4 -> 3, of which waited for: 4 -> 2; matrix products, arithmetic and copies ran while one was open for 4% -> 4% of each run, Pallas kernels for 0% -> 0%
where the time goes in v1:
time: 799 us; the launch traced here: 796 us
  waiting for transfers between devices  303 us (38%)
  local copies, waits for them, and re-layouts  167 us (21%)
  matrix products  125 us (16%)
  loops' own time  99.7 us (12%)
  other arithmetic  42.2 us (5%)
  blocking collectives  28.2 us (4%)
  starting transfers between devices  15.9 us (2%)
  between operations  14.3 us (2%)
    all_to_all x1, waiting for transfers between devices, per_device(): all_to_all(arr_next, concat_axis=0, split_axis=0, axis_name='seq')  281 us
    another operation x1, loops' own time, per_device(): lax.scan(one_block, carry, (key_blocks, value_blocks, jnp.arange(length /...  92.6 us
    dot_general x194, matrix products, softmax_update(): lax.dot_general(query[:, low:high], keys[:, low:high], (((1,), (1,)), (()...  63.9 us
    slice x96, local copies, waits for them, and re-layouts, visit(): positions[group][half - 1]  61.1 us
    dot_general x194, matrix products, softmax_update(): jnp.dot(probs.astype(jnp.bfloat16), values[:, low:high], preferred_elemen...  60.9 us
    squeeze x48, local copies, waits for them, and re-layouts, per_device(): lax.scan(one_block, carry, (key_blocks, value_blocks, jnp.arange(length /...  51.4 us
    reduce_sum x97, other arithmetic, softmax_update(): sums.append(totals[head] * shrink + jnp.sum(probs, axis=1))  35.5 us
    dynamic_slice x48, local copies, waits for them, and re-layouts, per_device(): lax.scan(one_block, carry, (key_blocks, value_blocks, jnp.arange(length /...  30.9 us
  transfers between devices with their start and end apart: 3, of which 2 were waited for; matrix products, arithmetic and copies ran while one was open for 4% of the time, Pallas kernels for 0%

profile of v1, /device:TPU:249, one launch (start us, length us, event | category | flops | bytes accessed | tf_op | source)
XLA Modules:
  0.0 795.7 jit_solution(5258924134853230812)
XLA Ops:
  7.2 3.9 copy.17
  11.1 4.1 all-to-all-start.1
  15.3 3.9 copy.19
  19.2 21.5 %all-to-all-done.1 = bf16[1024,4,256]{0,2,1:T(8,128)(2,1)S(1)} async-done(((bf16[1024,4,256]{0,2,1:T(8,128)(2,1)}), bf16[1024,4,256]{0,2,1:T(8,128)(2,1)S(1)}, u32[]{:S(2)}, u32[]{:S(2)}) %all-to-all-start.1) | async-done | bytes 2097184 | tf_op jit(solution)/shard_map/all_to_all | solution.py:121
  42.0 28.2 %all_to_all.43 = bf16[1024,4,256]{0,2,1:T(8,128)(2,1)S(1)} all-to-all(bf16[1024,4,256]{0,2,1:T(8,128)(2,1)} %bitcast.58), channel_id=1, replica_groups=mesh['seq'=64,'txt'=4] {'txt'}, dimensions={1} | all-to-all | bytes 4194304 | tf_op jit(solution)/shard_map/all_to_all | solution.py:122
  70.2 6.1 stack.12
  76.3 11.6 %all-to-all-start = ((bf16[64,384,256]{2,1,0:T(8,128)(2,1)}), bf16[64,384,256]{2,1,0:T(8,128)(2,1)}, u32[]{:S(2)}, u32[]{:S(2)}) async-start(bf16[64,384,256]{2,1,0:T(8,128)(2,1)} %stack.12), calls=%async_computation | async-start | bytes 25165824 | tf_op jit(solution)/shard_map/all_to_all | solution.py:100
  88.8 3.9 copy.18
  92.7 2.7 fusion.83
  96.8 3.3 fusion.48
  100.2 2.6 copy.20
  102.8 5.0 fusion.56
  107.8 4.5 fusion.59
  113.1 281.2 %all-to-all-done = bf16[64,384,256]{2,1,0:T(8,128)(2,1)} async-done(((bf16[64,384,256]{2,1,0:T(8,128)(2,1)}), bf16[64,384,256]{2,1,0:T(8,128)(2,1)}, u32[]{:S(2)}, u32[]{:S(2)}) %all-to-all-start) | async-done | bytes 12582944 | tf_op jit(solution)/shard_map/all_to_all | solution.py:100
  394.4 392.9 %while.20 = (s32[]{:T(128)}, f32[2,192]{1,0:T(2,128)S(1)}, f32[2,192]{1,0:T(2,128)S(1)}, f32[192,256]{1,0:T(8,128)S(1)}, f32[2,192]{1,0:T(2,128)S(1)}, /*index=5...) while((s32[]{:T(128)}, f32[2,192]{1,0:T(2,128)S(1)}, ...), condition=%wide.region_13.14_spmd, body=%wide.region_0.13_spmd.sunk | while | flops 206148608 | bytes 8684497 | solution.py:112
  398.1 1.6 conditional.5
  401.0 1.6 conditional.4
  406.2 1.6 conditional.5
  417.3 1.6 conditional.4
  425.5 1.6 conditional.4
  433.7 1.6 conditional.4
  441.9 1.6 conditional.4
  450.1 1.6 conditional.4
  458.3 1.6 conditional.4
  466.4 1.6 conditional.4
  474.6 1.6 conditional.4
  482.8 1.6 conditional.4
  491.0 1.6 conditional.4
  499.2 1.6 conditional.4
  507.4 1.6 conditional.4
  515.5 1.6 conditional.4
  523.7 1.6 conditional.4
  531.9 1.6 conditional.4
  540.1 1.6 conditional.4
  548.3 1.6 conditional.4
  556.5 1.6 conditional.4
  564.7 1.6 conditional.4
  572.8 1.6 conditional.4
  581.0 1.6 conditional.4
  589.2 1.6 conditional.4
  597.4 1.6 conditional.4
  605.6 1.6 conditional.4
  613.8 1.6 conditional.4
  622.0 1.6 conditional.4
  630.1 1.6 conditional.4
  638.3 1.6 conditional.4
  646.5 1.6 conditional.4
  654.7 1.6 conditional.4
  662.9 1.6 conditional.4
  671.1 1.6 conditional.4
  679.3 1.6 conditional.4
  687.4 1.6 conditional.4
  695.6 1.6 conditional.4
  703.8 1.6 conditional.4
  712.0 1.6 conditional.4
  720.2 1.6 conditional.4
  728.4 1.6 conditional.4
  736.5 1.6 conditional.4
  744.7 1.6 conditional.4
  752.9 1.6 conditional.4
  761.1 1.6 conditional.4
  769.3 1.6 conditional.4
  777.5 1.6 conditional.4
  785.7 1.6 conditional.4
  (1393 shorter events, 375.8 us)
Async XLA Ops:
  11.1 59.1 %copy-start.6 = (bf16[384,256]{1,0:T(8,128)(2,1)S(1)}, bf16[384,256]{1,0:T(8,128)(2,1)}, u32[]{:S(2)}) copy-start(bf16[384,256]{1,0:T(8,128)(2,1)} %param.15) | copy-start | bytes 589828
  11.1 29.6 %all-to-all-start.1 = ((bf16[1024,4,256]{0,2,1:T(8,128)(2,1)}), bf16[1024,4,256]{0,2,1:T(8,128)(2,1)S(1)}, u32[]{:S(2)}, u32[]{:S(2)}) async-start(bf16[1024,4,256]{0,2,1:T(8,128)(2,1)} %bitcast.57), calls=%async_computation.1 | async-start | bytes 4194304 | tf_op jit(solution)/shard_map/all_to_all | solution.py:121
  40.7 1.3 copy-start
  76.3 12.3 %copy-start.8 = (s32[3]{0:T(128)S(1)}, s32[3]{0:T(128)}, u32[]{:S(2)}) copy-start(s32[3]{0:T(128)} %param.19) | copy-start | bytes 40
  76.3 12.4 %copy-start.5 = (bf16[384,256]{1,0:T(8,128)(2,1)S(1)}, bf16[384,256]{1,0:T(8,128)(2,1)}, u32[]{:S(2)}) copy-start(bf16[384,256]{1,0:T(8,128)(2,1)} %param.13) | copy-start | bytes 589828
  76.3 16.4 %copy-start.7 = (bf16[384,256]{1,0:T(8,128)(2,1)S(1)}, bf16[384,256]{1,0:T(8,128)(2,1)}, u32[]{:S(2)}) copy-start(bf16[384,256]{1,0:T(8,128)(2,1)} %param.16) | copy-start | bytes 589828
  76.3 318.0 %all-to-all-start = ((bf16[64,384,256]{2,1,0:T(8,128)(2,1)}), bf16[64,384,256]{2,1,0:T(8,128)(2,1)}, u32[]{:S(2)}, u32[]{:S(2)}) async-start(bf16[64,384,256]{2,1,0:T(8,128)(2,1)} %stack.12), calls=%async_computation | async-start | bytes 25165824 | tf_op jit(solution)/shard_map/all_to_all | solution.py:100
  87.9 306.4 %all-gather.2.cloned.1.call-start = ((), (), s32[]{:S(2)}) async-start(), calls=%async_computation.3 | async-start | bytes 12779520 | tf_op jit(solution)/shard_map/all_gather | solution.py:97
  92.7 2.7 copy-start.4
  95.4 4.7 copy-start.1
  96.8 3.3 copy-start.2
  102.8 5.0 copy-start.3
Sparse Core Ops, SparseCore 0:
  91.5 172.7 all-gather.1
